TPU v7x, 512 devices: a whole 4x8x8 slice. The times are simulated.
512 devices in a mesh: dp: 4 (over x), shard: 128 (over z, y, core).
Axes of the slice: x: 4, y: 8, z: 8, core: 2. Of those that a mesh axis runs over, the one named last changes fastest.
Arguments:
- grad_parts: float32 [4, 1024, 16384], P('dp', None, 'shard'), may hold values from -0.3 to 0.3
- owner: int32 [1024], replicated, may hold values from 0 to 127, as said below
- master: float32 [4, 128, 4, 128, 128], P('dp', 'shard'), may hold values from -6 to 6
- first_moment: float32 [4, 128, 4, 128, 128], P('dp', 'shard'), may hold values from -0.12 to 0.12
- second_moment: float32 [4, 128, 4, 128, 128], P('dp', 'shard'), may hold values from 0.0001 to 0.001
- left_stat: float32 [4, 128, 4, 128, 128], P('dp', 'shard'), may hold values from -0.0062992126 to 10
- right_stat: float32 [4, 128, 4, 128, 128], P('dp', 'shard'), may hold values from -0.0062992126 to 10
- left_basis: float32 [4, 128, 4, 128, 128], P('dp', 'shard'), may hold values from -0.079549513 to 1.0795495
- right_basis: float32 [4, 128, 4, 128, 128], P('dp', 'shard'), may hold values from -0.079549513 to 1.0795495
Outputs:
- new_params: bfloat16 [1024, 16384], P(None, 'shard')
- master_out: float32 [4, 128, 4, 128, 128], P('dp', 'shard')
- first_out: float32 [4, 128, 4, 128, 128], P('dp', 'shard')
- second_out: float32 [4, 128, 4, 128, 128], P('dp', 'shard')
- left_stat_out: float32 [4, 128, 4, 128, 128], P('dp', 'shard')
- right_stat_out: float32 [4, 128, 4, 128, 128], P('dp', 'shard')
- left_basis_out: float32 [4, 128, 4, 128, 128], P('dp', 'shard')
- right_basis_out: float32 [4, 128, 4, 128, 128], P('dp', 'shard')
Inputs may be any that keep to these rules, and one draw needn't show every extreme that they name: In each group of 256 consecutive tiles no owner index holds more than 4 tiles, and some owner holds exactly 4.
All inputs are finite; a program needn't handle non-finite values.
Results may differ from a plain program's by a relative error of at most 0.001.
Values may be sent and summed in bfloat16 or wider, within the bound.
No kernel may reach another device: no remote copies, remote signals or barrier semaphores. Data moves between devices by JAX's collectives and lax.ppermute only.
A program may use at most 64 MiB of HBM per device.

v0:
```python
import jax
import jax.numpy as jnp
from jax import lax
from jax.sharding import PartitionSpec as P

NS_STEPS = 10
beta_one = 0.9
beta_two = 0.95
stat_decay = 0.95
learn_rate = 0.05
weight_decay = 0.01
adam_eps = 1e-08
highest = lax.Precision.HIGHEST


def product(form, left, right):
    return jnp.einsum(form, left, right, precision=highest)


def slot_index(owners, shards):
    matches = (owners[..., None] == jnp.arange(shards, dtype=jnp.int32)).astype(jnp.int32)
    running = jnp.cumsum(matches, axis=1)
    return jnp.sum(matches * running, axis=-1) - 1


def orthogonal(pending):
    iterate = pending * lax.rsqrt(jnp.sum(pending * pending, axis=(1, 2), keepdims=True) + 1e-06)
    for step in range(NS_STEPS):
        gram = product("nik,njk->nij", iterate, iterate)
        iterate = 1.5 * iterate - 0.5 * product("nij,njk->nik", gram, iterate)
    return iterate


def soap_update(gradient, master, first, second, lstat, rstat, lbasis, rbasis):
    first_new = beta_one * first + (1.0 - beta_one) * gradient
    grad_rot = product("nik,nkl->nil", product("nji,njk->nik", lbasis, gradient), rbasis)
    first_rot = product("nik,nkl->nil", product("nji,njk->nik", lbasis, first_new), rbasis)
    second_new = beta_two * second + (1.0 - beta_two) * grad_rot * grad_rot
    normed = first_rot / (jnp.sqrt(second_new) + adam_eps)
    update = product("nik,nlk->nil", product("nij,njk->nik", lbasis, normed), rbasis)
    master_new = master - learn_rate * (update + weight_decay * master)
    lstat_new = stat_decay * lstat + (1.0 - stat_decay) * product(
        "nik,njk->nij", gradient, gradient
    )
    rstat_new = stat_decay * rstat + (1.0 - stat_decay) * product(
        "nki,nkj->nij", gradient, gradient
    )
    lbasis_new = orthogonal(product("nij,njk->nik", lstat_new, lbasis))
    rbasis_new = orthogonal(product("nij,njk->nik", rstat_new, rbasis))
    return (master_new, first_new, second_new, lstat_new, rstat_new, lbasis_new, rbasis_new)


def body(
    grad_parts,
    owner,
    master,
    first_moment,
    second_moment,
    left_stat,
    right_stat,
    left_basis,
    right_basis,
):
    shards = lax.axis_size("shard")
    groups = lax.axis_size("dp")
    my_group = lax.axis_index("dp")
    capacity = master.shape[2]
    block_size = master.shape[4]
    piece_len = grad_parts.shape[2]
    tile_count = owner.shape[0]
    per_group = tile_count // groups
    owners = owner.reshape(groups, per_group)
    place_index = slot_index(owners, shards) * shards + owners
    own_place = lax.dynamic_index_in_dim(place_index, my_group, 0, keepdims=False)
    summed = lax.psum_scatter(grad_parts, "dp", scatter_dimension=1, tiled=True)
    outgoing = jnp.zeros((capacity * shards, piece_len), jnp.float32)
    outgoing = outgoing.at[own_place].set(summed[0])
    outgoing = outgoing.reshape(capacity, shards, piece_len)
    incoming = lax.all_to_all(outgoing, "shard", split_axis=1, concat_axis=1, tiled=True)

    def as_tiles(array):
        return array.reshape(capacity, block_size, block_size)

    results = soap_update(
        incoming,
        as_tiles(master),
        as_tiles(first_moment),
        as_tiles(second_moment),
        as_tiles(left_stat),
        as_tiles(right_stat),
        as_tiles(left_basis),
        as_tiles(right_basis),
    )
    shaped = [item.reshape(1, 1, capacity, block_size, block_size) for item in results]
    weights = results[0].astype(jnp.bfloat16)
    returned = lax.all_to_all(weights, "shard", split_axis=1, concat_axis=1, tiled=True)
    returned = returned.reshape(capacity * shards, piece_len)
    own_rows = returned[own_place]
    new_params = lax.all_gather(own_rows, "dp", axis=0, tiled=True)
    return (new_params, shaped[0], shaped[1], shaped[2], shaped[3], shaped[4], shaped[5], shaped[6])


def solution(mesh):
    placed = (
        P("dp", None, "shard"),
        P(),
        P("dp", "shard", None, None, None),
        P("dp", "shard", None, None, None),
        P("dp", "shard", None, None, None),
        P("dp", "shard", None, None, None),
        P("dp", "shard", None, None, None),
        P("dp", "shard", None, None, None),
        P("dp", "shard", None, None, None),
    )
    return jax.shard_map(
        body,
        mesh=mesh,
        in_specs=placed,
        out_specs=(
            P(None, "shard"),
            P("dp", "shard", None, None, None),
            P("dp", "shard", None, None, None),
            P("dp", "shard", None, None, None),
            P("dp", "shard", None, None, None),
            P("dp", "shard", None, None, None),
            P("dp", "shard", None, None, None),
            P("dp", "shard", None, None, None),
        ),
        check_vma=False,
    )
```

profile of v0, /device:TPU:8, one launch (start us, length us, event | category | flops | bytes accessed | tf_op | source)
XLA Modules:
  0.0 143.0 jit_solution(8679170944378737934)
XLA Ops:
  7.2 0.7 reduce-scatter.2.cloned.1.call-update
  7.9 0.7 copy-done.10
  8.8 0.9 fusion.26
  10.3 31.9 %reduce-scatter.2.cloned.1.call-done = f32[1,256,128]{2,1,0:T(8,128)} async-done(((f32[1,1024,128]{2,1,0:T(8,128)}), f32[1,256,128]{2,1,0:T(8,128)}) %reduce-scatter.2.cloned.1.call-update) | async-done | bytes 131088 | tf_op jit(solution)/shard_map/reduce_scatter | solution.py:75
  42.2 1.6 %scatter_custom_fusion = f32[512,128]{1,0:T(8,128)S(1)} fusion(s32[256]{0:T(256)S(1)} %bitcast.159, f32[1,256,128]{2,1,0:T(8,128)} %reduce-scatter.2.cloned.1.call-done, f32[]{:T(128)} %constant.18.clone.1), kind=kCustom, calls=%fused_computation.91 | custom fusion | bytes 393220 | tf_op jit(solution)/shard_map/scatter | solution.py:77
  43.8 0.9 copy.40
  44.7 14.5 %all-to-all-start = ((f32[4,128,128]{2,0,1:T(4,128)}), f32[4,128,128]{2,0,1:T(4,128)S(1)}, u32[]{:S(2)}, u32[]{:S(2)}) async-start(f32[4,128,128]{2,0,1:T(4,128)} %copy.40), calls=%async_computation.1 | async-start | bytes 524288 | tf_op jit(solution)/shard_map/all_to_all | solution.py:79
  59.2 14.5 %all-to-all-done = f32[4,128,128]{2,0,1:T(4,128)S(1)} async-done(((f32[4,128,128]{2,0,1:T(4,128)}), f32[4,128,128]{2,0,1:T(4,128)S(1)}, u32[]{:S(2)}, u32[]{:S(2)}) %all-to-all-start) | async-done | bytes 262176 | tf_op jit(solution)/shard_map/all_to_all | solution.py:79
  74.9 0.8 fusion.51
  77.2 0.7 fusion.77
  78.3 0.7 fusion.78
  79.4 0.7 fusion.79
  80.4 0.7 fusion.80
  81.5 0.7 fusion.81
  82.6 0.7 fusion.82
  83.7 0.7 fusion.83
  84.8 0.7 fusion.84
  88.0 0.8 fusion.54
  90.3 0.8 fusion.68
  91.6 0.7 fusion.69
  94.8 0.7 fusion.72
  95.9 0.7 fusion.73
  102.0 1.4 fusion.66
  103.4 0.8 copy.47
  104.1 6.1 %all-to-all-start.1 = ((bf16[4,128,128]{2,0,1:T(4,128)(2,1)}), bf16[4,128,128]{2,0,1:T(4,128)(2,1)S(1)}, u32[]{:S(2)}, u32[]{:S(2)}) async-start(bf16[4,128,128]{2,0,1:T(4,128)(2,1)} %copy.47), calls=%async_computation.2 | async-start | bytes 262144 | tf_op jit(solution)/shard_map/all_to_all | solution.py:96
  110.2 0.7 copy.53
  111.0 1.1 fusion.1
  112.1 1.1 fusion.12
  113.2 9.1 %all-to-all-done.1 = bf16[4,128,128]{2,0,1:T(4,128)(2,1)S(1)} async-done(((bf16[4,128,128]{2,0,1:T(4,128)(2,1)}), bf16[4,128,128]{2,0,1:T(4,128)(2,1)S(1)}, u32[]{:S(2)}, u32[]{:S(2)}) %all-to-all-start.1) | async-done | bytes 131104 | tf_op jit(solution)/shard_map/all_to_all | solution.py:96
  122.3 0.9 gather_fusion
  123.2 12.3 %all-gather = bf16[1024,128]{1,0:T(8,128)(2,1)S(1)} all-gather(bf16[256,128]{1,0:T(8,128)(2,1)S(1)} %gather_fusion), channel_id=2, replica_groups=mesh['dp'=4,'shard'=128] {'dp'}, dimensions={0}, use_global_device_ids=true | all-gather | bytes 327680 | tf_op jit(solution)/shard_map/all_gather | solution.py:99
  135.5 0.7 copy.69
  (71 shorter events, 19.3 us)
Async XLA Ops:
  7.2 67.0 %copy-start = (f32[1,1,4,128,128]{4,3,2,1,0:T(8,128)S(1)}, f32[1,1,4,128,128]{4,3,2,1,0:T(8,128)}, u32[]{:S(2)}) copy-start(f32[1,1,4,128,128]{4,3,2,1,0:T(8,128)} %param.17) | copy-start | bytes 786436
  7.2 35.0 %reduce-scatter.2.cloned.1.call-start = ((), (), s32[]{:S(2)}) async-start(), calls=%async_computation.3 | async-start | bytes 655360 | tf_op jit(solution)/shard_map/reduce_scatter | solution.py:75
  7.9 0.7 copy-start.10
  44.6 14.5 %copy-start.6 = (f32[1,1,4,128,128]{4,3,2,1,0:T(8,128)S(1)}, f32[1,1,4,128,128]{4,3,2,1,0:T(8,128)}, u32[]{:S(2)}) copy-start(f32[1,1,4,128,128]{4,3,2,1,0:T(8,128)} %param.12) | copy-start | bytes 786436
  44.7 29.0 %all-to-all-start = ((f32[4,128,128]{2,0,1:T(4,128)}), f32[4,128,128]{2,0,1:T(4,128)S(1)}, u32[]{:S(2)}, u32[]{:S(2)}) async-start(f32[4,128,128]{2,0,1:T(4,128)} %copy.40), calls=%async_computation.1 | async-start | bytes 524288 | tf_op jit(solution)/shard_map/all_to_all | solution.py:79
  59.2 14.6 %copy-start.7 = (f32[1,1,4,128,128]{4,3,2,1,0:T(8,128)S(1)}, f32[1,1,4,128,128]{4,3,2,1,0:T(8,128)}, u32[]{:S(2)}) copy-start(f32[1,1,4,128,128]{4,3,2,1,0:T(8,128)} %param.15) | copy-start | bytes 786436
  74.2 0.7 copy-start.3
  84.8 1.0 copy-start.1
  85.7 0.9 copy-start.5
  87.3 0.7 copy-start.2
  99.0 1.0 copy-start.8
  100.3 0.7 copy-start.4
  101.1 0.9 copy-start.9
  104.1 18.2 %all-to-all-start.1 = ((bf16[4,128,128]{2,0,1:T(4,128)(2,1)}), bf16[4,128,128]{2,0,1:T(4,128)(2,1)S(1)}, u32[]{:S(2)}, u32[]{:S(2)}) async-start(bf16[4,128,128]{2,0,1:T(4,128)(2,1)} %copy.47), calls=%async_computation.2 | async-start | bytes 262144 | tf_op jit(solution)/shard_map/all_to_all | solution.py:96
Sparse Core Ops, SparseCore 0:
  10.8 31.2 reduce-scatter.1
where the time goes:
time: 143 us
  waiting for transfers between devices  56.1 us (39%)
  matrix products  28.9 us (20%)
  starting transfers between devices  20.6 us (14%)
  between operations  14.6 us (10%)
  blocking collectives  12.3 us (9%)
  local copies, waits for them, and re-layouts  8.78 us (6%)
  other arithmetic  1.75 us (1%)
    reduce_scatter x1, waiting for transfers between devices, body(): summed = lax.psum_scatter(grad_parts, 'dp', scatter_dimension=1, tiled=True)  31.9 us
    dot_general x50, matrix products, product(): return jnp.einsum(form, left, right, precision=highest)  28.9 us
    all_to_all x1, waiting for transfers between devices, body(): lax.all_to_all(outgoing, 'shard', split_axis=1, concat_axis=1, tiled=True)  14.5 us
    all_to_all x1, starting transfers between devices, body(): lax.all_to_all(outgoing, 'shard', split_axis=1, concat_axis=1, tiled=True)  14.5 us
    all_gather x1, blocking collectives, body(): new_params = lax.all_gather(own_rows, 'dp', axis=0, tiled=True)  12.3 us
    all_to_all x1, waiting for transfers between devices, body(): lax.all_to_all(weights, 'shard', split_axis=1, concat_axis=1, tiled=True)  9.13 us
    all_to_all x1, starting transfers between devices, body(): lax.all_to_all(weights, 'shard', split_axis=1, concat_axis=1, tiled=True)  6.1 us
    unnamed x24, local copies, waits for them, and re-layouts  4.36 us
  transfers between devices with their start and end apart: 3, of which 3 were waited for; matrix products, arithmetic and copies ran while one was open for 3% of the time, Pallas kernels for 0%

commit v1 on v0

--- a/solution.py
+++ b/solution.py
@@ -76,7 +76,16 @@
     outgoing = jnp.zeros((capacity * shards, piece_len), jnp.float32)
     outgoing = outgoing.at[own_place].set(summed[0])
     outgoing = outgoing.reshape(capacity, shards, piece_len)
-    incoming = lax.all_to_all(outgoing, "shard", split_axis=1, concat_axis=1, tiled=True)
+    start_circles = lambda xx: jnp.concatenate(
+        jax.lax.all_to_all(
+            jnp.stack(jnp.split(xx, jax.lax.psum(1, axis_name="shard"), axis=1)),
+            axis_name="shard",
+            split_axis=0,
+            concat_axis=0,
+        ),
+        axis=1,
+    )
+    incoming = start_circles(outgoing)
 
     def as_tiles(array):
         return array.reshape(capacity, block_size, block_size)

time: 143 us -> 217 us (1.52)
  local copies, waits for them, and re-layouts: 8.78 us -> 82.9 us
    unnamed x24 -> x152, local copies, waits for them, and re-layouts: 4.36 us -> 78.5 us
  transfers between devices with their start and end apart: 3 -> 3, of which waited for: 3 -> 3; matrix products, arithmetic and copies ran while one was open for 3% -> 2% of each run, Pallas kernels for 0% -> 0%
where the time goes in v1:
time: 217 us
  local copies, waits for them, and re-layouts  82.9 us (38%)
  waiting for transfers between devices  55.9 us (26%)
  matrix products  29.1 us (13%)
  starting transfers between devices  20.6 us (9%)
  between operations  14.7 us (7%)
  blocking collectives  12.3 us (6%)
    unnamed x152, local copies, waits for them, and re-layouts  78.5 us
    reduce_scatter x1, waiting for transfers between devices, body(): summed = lax.psum_scatter(grad_parts, 'dp', scatter_dimension=1, tiled=True)  31.9 us
    dot_general x50, matrix products, product(): return jnp.einsum(form, left, right, precision=highest)  29.1 us
    all_to_all x1, starting transfers between devices, body(): jax.lax.all_to_all(jnp.stack(jnp.split(xx, jax.lax.psum(1, axis_name='sha...  14.5 us
    all_to_all x1, waiting for transfers between devices, body(): jax.lax.all_to_all(jnp.stack(jnp.split(xx, jax.lax.psum(1, axis_name='sha...  14.4 us
    all_gather x1, blocking collectives, body(): new_params = lax.all_gather(own_rows, 'dp', axis=0, tiled=True)  12.3 us
    all_to_all x1, waiting for transfers between devices, body(): lax.all_to_all(weights, 'shard', split_axis=1, concat_axis=1, tiled=True)  9.02 us
    all_to_all x1, starting transfers between devices, body(): lax.all_to_all(weights, 'shard', split_axis=1, concat_axis=1, tiled=True)  6.1 us
  transfers between devices with their start and end apart: 3, of which 3 were waited for; matrix products, arithmetic and copies ran while one was open for 2% of the time, Pallas kernels for 0%

profile of v1, /device:TPU:8, one launch (start us, length us, event | category | flops | bytes accessed | tf_op | source)
XLA Modules:
  0.0 217.0 jit_solution(11143990003572073373)
XLA Ops:
  7.2 0.7 reduce-scatter.2.cloned.1.call-update
  7.9 0.7 copy-done.10
  8.8 0.9 fusion.26
  10.3 31.9 %reduce-scatter.2.cloned.1.call-done = f32[1,256,128]{2,1,0:T(8,128)} async-done(((f32[1,1024,128]{2,1,0:T(8,128)}), f32[1,256,128]{2,1,0:T(8,128)}) %reduce-scatter.2.cloned.1.call-update) | async-done | bytes 131088 | tf_op jit(solution)/shard_map/reduce_scatter | solution.py:75
  42.2 1.6 scatter_custom_fusion
  118.2 14.5 %all-to-all-start = ((f32[128,4,1,128]{3,1,2,0:T(4,128)}), f32[128,4,1,128]{3,1,2,0:T(4,128)S(1)}, u32[]{:S(2)}, u32[]{:S(2)}) async-start(f32[128,4,1,128]{3,1,2,0:T(4,128)} %constant_dynamic-update-slice_fusion), calls=%async_computation.1 | async-start | bytes 524288 | tf_op jit(solution)/shard_map/all_to_all | solution.py:80
  132.8 14.4 %all-to-all-done = f32[128,4,1,128]{3,1,2,0:T(4,128)S(1)} async-done(((f32[128,4,1,128]{3,1,2,0:T(4,128)}), f32[128,4,1,128]{3,1,2,0:T(4,128)S(1)}, u32[]{:S(2)}, u32[]{:S(2)}) %all-to-all-start) | async-done | bytes 262176 | tf_op jit(solution)/shard_map/all_to_all | solution.py:80
  148.5 0.9 copy-done.5
  149.4 0.7 fusion.22
  150.8 0.8 fusion.53
  152.0 0.7 fusion.90
  153.1 0.7 fusion.91
  154.2 0.7 fusion.92
  155.3 0.7 fusion.93
  156.3 0.7 fusion.94
  157.4 0.7 fusion.95
  158.5 0.7 fusion.96
  159.6 0.7 fusion.97
  162.9 0.8 fusion.56
  164.1 0.9 fusion.81
  165.4 0.7 fusion.82
  170.8 0.7 fusion.87
  176.0 1.4 fusion.80
  177.4 0.8 copy.411
  178.1 6.1 %all-to-all-start.1 = ((bf16[4,128,128]{2,0,1:T(4,128)(2,1)}), bf16[4,128,128]{2,0,1:T(4,128)(2,1)S(1)}, u32[]{:S(2)}, u32[]{:S(2)}) async-start(bf16[4,128,128]{2,0,1:T(4,128)(2,1)} %copy.411), calls=%async_computation.2 | async-start | bytes 262144 | tf_op jit(solution)/shard_map/all_to_all | solution.py:105
  184.2 0.8 copy.416
  185.1 1.1 fusion.1
  186.2 1.1 fusion.12
  187.3 9.0 %all-to-all-done.1 = bf16[4,128,128]{2,0,1:T(4,128)(2,1)S(1)} async-done(((bf16[4,128,128]{2,0,1:T(4,128)(2,1)}), bf16[4,128,128]{2,0,1:T(4,128)(2,1)S(1)}, u32[]{:S(2)}, u32[]{:S(2)}) %all-to-all-start.1) | async-done | bytes 131104 | tf_op jit(solution)/shard_map/all_to_all | solution.py:105
  196.3 0.9 gather_fusion
  197.2 12.3 %all-gather = bf16[1024,128]{1,0:T(8,128)(2,1)S(1)} all-gather(bf16[256,128]{1,0:T(8,128)(2,1)S(1)} %gather_fusion), channel_id=2, replica_groups=mesh['dp'=4,'shard'=128] {'dp'}, dimensions={0}, use_global_device_ids=true | all-gather | bytes 327680 | tf_op jit(solution)/shard_map/all_gather | solution.py:108
  209.5 0.7 copy.685
  (205 shorter events, 93.2 us)
Async XLA Ops:
  7.2 142.9 %copy-start = (f32[1,1,4,128,128]{4,3,2,1,0:T(8,128)S(1)}, f32[1,1,4,128,128]{4,3,2,1,0:T(8,128)}, u32[]{:S(2)}) copy-start(f32[1,1,4,128,128]{4,3,2,1,0:T(8,128)} %param.17) | copy-start | bytes 786436
  7.2 35.0 %reduce-scatter.2.cloned.1.call-start = ((), (), s32[]{:S(2)}) async-start(), calls=%async_computation.3 | async-start | bytes 655360 | tf_op jit(solution)/shard_map/reduce_scatter | solution.py:75
  7.9 0.7 copy-start.10
  118.2 14.5 %copy-start.7 = (f32[1,1,4,128,128]{4,3,2,1,0:T(8,128)S(1)}, f32[1,1,4,128,128]{4,3,2,1,0:T(8,128)}, u32[]{:S(2)}) copy-start(f32[1,1,4,128,128]{4,3,2,1,0:T(8,128)} %param.12) | copy-start | bytes 786436
  118.2 29.0 %all-to-all-start = ((f32[128,4,1,128]{3,1,2,0:T(4,128)}), f32[128,4,1,128]{3,1,2,0:T(4,128)S(1)}, u32[]{:S(2)}, u32[]{:S(2)}) async-start(f32[128,4,1,128]{3,1,2,0:T(4,128)} %constant_dynamic-update-slice_fusion), calls=%async_computation.1 | async-start | bytes 524288 | tf_op jit(solution)/shard_map/all_to_all | solution.py:80
  132.8 14.5 %copy-start.1 = (f32[1,1,4,128,128]{4,3,2,1,0:T(8,128)S(1)}, f32[1,1,4,128,128]{4,3,2,1,0:T(8,128)}, u32[]{:S(2)}) copy-start(f32[1,1,4,128,128]{4,3,2,1,0:T(8,128)} %param.16) | copy-start | bytes 786436
  148.5 1.0 copy-start.5
  150.1 0.7 copy-start.2
  160.7 1.0 copy-start.6
  162.2 0.7 copy-start.3
  172.9 1.0 copy-start.8
  174.3 0.7 copy-start.4
  175.0 0.9 copy-start.9
  178.1 18.2 %all-to-all-start.1 = ((bf16[4,128,128]{2,0,1:T(4,128)(2,1)}), bf16[4,128,128]{2,0,1:T(4,128)(2,1)S(1)}, u32[]{:S(2)}, u32[]{:S(2)}) async-start(bf16[4,128,128]{2,0,1:T(4,128)(2,1)} %copy.411), calls=%async_computation.2 | async-start | bytes 262144 | tf_op jit(solution)/shard_map/all_to_all | solution.py:105
Sparse Core Ops, SparseCore 0:
  10.8 31.2 reduce-scatter.1
